TPU v7x, 32 devices: a whole 2x2x4 slice. The times are simulated.
32 devices in a mesh: section: 2 (over x), fsdp: 4 (over z), dp: 4 (over y, core).
Axes of the slice: x: 2, y: 2, z: 4, core: 2. Of those that a mesh axis runs over, the one named last changes fastest.
Arguments:
- activations: bfloat16 [2, 4, 512, 3584], P('section', None, ('fsdp', 'dp')), may hold values from -6 to 6
- out_grad: bfloat16 [2, 4, 512, 14336], P('section', None, ('fsdp', 'dp')), may hold values from -6 to 6
- blocks: bfloat16 [2, 16, 128, 128], P('section', 'fsdp'), may hold values from -0.5 to 0.5
- pattern: int32 [2, 16, 2], P('section', 'fsdp'), may hold values from 0 to 111, as said below
- order: int32 [4], replicated, may hold values from 0 to 3, each once
Outputs:
- received: bfloat16 [2, 4, 512, 3584], P('section', None, ('fsdp', 'dp'))
- weight_grad: float32 [2, 16, 128, 128], P('section', 'fsdp')
Inputs may be any that keep to these rules, and one draw needn't show every extreme that they name: pattern[s, b, 0] < 28 and pattern[s, b, 1] < 112; no two blocks of one section share both indices; within a section the blocks stand in ascending order of (row, column). `order`: a permutation of the microbatches.
All inputs are finite; a program needn't handle non-finite values.
Results may differ from a plain program's by a relative error of at most 0.0049.
Values may be sent and summed in bfloat16 or wider, within the bound.
No kernel may reach another device: no remote copies, remote signals or barrier semaphores. Data moves between devices by JAX's collectives and lax.ppermute only.
A program may use at most 128 MiB of HBM per device.

v0:
```python
import math
import jax
import jax.numpy as jnp
from jax import lax
from jax.sharding import PartitionSpec as P


def passed_along(block, axis, distance):
    devices = range(lax.axis_size(axis))
    route = [(i - distance, i) for i in devices if i - distance in devices]
    return lax.ppermute(block, axis, route)


def silu_slope(pre_act):
    sigmoid_val = jax.nn.sigmoid(pre_act)
    return sigmoid_val * (1.0 + pre_act * (1.0 - sigmoid_val))


def in_groups(step_fn, running, shard_blocks, first_block):
    block_count = shard_blocks.shape[0]
    group_size = math.gcd(block_count, 32)
    if group_size == block_count:
        return step_fn(running, shard_blocks, first_block)

    def one_group(number, carried):
        segment = lax.dynamic_slice_in_dim(shard_blocks, number * group_size, group_size, 0)
        return step_fn(carried, segment, first_block + number * group_size)

    return lax.fori_loop(0, block_count // group_size, one_group, running)


def local(activations, out_grad, blocks, pattern, order):
    block_size = blocks.shape[-1]
    micro_count = activations.shape[1]
    tok_rows = activations.shape[1] * activations.shape[2]
    row_count = activations.shape[3] // block_size
    col_count = out_grad.shape[3] // block_size
    features = activations[0].reshape(tok_rows, row_count, block_size)
    hidden_grad = out_grad[0].reshape(tok_rows, out_grad.shape[3])
    own_blocks = blocks[0]
    all_indices = lax.all_gather(pattern[0], "fsdp", axis=0, tiled=True)

    def forward_step(running, shard_blocks, first_block):
        indices = lax.dynamic_slice_in_dim(all_indices, first_block, shard_blocks.shape[0], 0)
        rows_in = jnp.take(features, indices[:, 0], axis=1)
        product = jnp.einsum(
            "tbk,bkn->tbn", rows_in, shard_blocks, preferred_element_type=jnp.float32
        )
        return running.at[:, indices[:, 1]].add(product)

    pre_zero = jnp.zeros((tok_rows, col_count, block_size), jnp.float32)
    pre_act = in_groups(
        forward_step, pre_zero, lax.all_gather(own_blocks, "fsdp", axis=0, tiled=True), jnp.int32(0)
    )
    act_grad = (hidden_grad.astype(jnp.float32) * silu_slope(pre_act.reshape(tok_rows, -1))).astype(
        jnp.bfloat16
    )
    grad_cols = act_grad.reshape(tok_rows, col_count, block_size)

    def backward_step(running, shard_blocks, first_block):
        indices = lax.dynamic_slice_in_dim(all_indices, first_block, shard_blocks.shape[0], 0)
        cols_in = jnp.take(grad_cols, indices[:, 1], axis=1)
        product = jnp.einsum(
            "tbn,bkn->tbk", cols_in, shard_blocks, preferred_element_type=jnp.float32
        )
        return running.at[:, indices[:, 0]].add(product)

    back_zero = jnp.zeros((tok_rows, row_count, block_size), jnp.float32)
    input_grad = in_groups(
        backward_step,
        back_zero,
        lax.all_gather(own_blocks, "fsdp", axis=0, tiled=True),
        jnp.int32(0),
    )
    input_grad = input_grad.astype(jnp.bfloat16).reshape(
        micro_count, activations.shape[2], activations.shape[3]
    )
    ordered = jnp.take(input_grad, order, axis=0)
    received = passed_along(ordered, "section", -1)
    indices = all_indices
    rows_in = jnp.take(features, indices[:, 0], axis=1)
    cols_in = jnp.take(grad_cols, indices[:, 1], axis=1)
    owned_grads = lax.psum_scatter(
        jnp.einsum("tbk,tbn->bkn", rows_in, cols_in, preferred_element_type=jnp.float32),
        "fsdp",
        scatter_dimension=0,
        tiled=True,
    )
    summed = lax.psum(owned_grads, "dp")
    grad_scale = 1.0 / math.sqrt(tok_rows * lax.axis_size("fsdp") * lax.axis_size("dp"))
    return (received[None], (summed * grad_scale)[None])


def solution(mesh):
    in_specs = (
        P("section", None, ("fsdp", "dp"), None),
        P("section", None, ("fsdp", "dp"), None),
        P("section", "fsdp", None, None),
        P("section", "fsdp", None),
        P(),
    )
    out_specs = (P("section", None, ("fsdp", "dp"), None), P("section", "fsdp", None, None))
    return jax.shard_map(local, mesh=mesh, in_specs=in_specs, out_specs=out_specs, check_vma=False)
```

profile of v0, /device:TPU:0, one launch (start us, length us, event | category | flops | bytes accessed | tf_op | source)
XLA Modules:
  0.0 135.6 jit_solution(16365849403868641486)
XLA Ops:
  7.2 0.0 reduce-scatter.2.cloned.1.call-start
  7.2 0.8 copy.12
  8.0 13.6 %all-gather = s32[1,16,2]{2,0,1:T(1,128)S(1)} all-gather(s32[1,4,2]{2,0,1:T(1,128)S(1)} %copy.12), channel_id=2, replica_groups=mesh['section'=2,'fsdp'=4,'dp'=4] {'fsdp'}, dimensions={1}, use_global_device_ids=true | all-gather | bytes 160 | tf_op jit(solution)/shard_map/all_gather | solution.py:41
  21.6 0.1 copy.13
  21.7 1.6 %reshape_squeeze.4 = bf16[128,28,128]{2,1,0:T(8,128)(2,1)S(1)} reshape(bf16[1,4,32,3584]{3,2,1,0:T(8,128)(2,1)} %param.9) | data formatting | bytes 1835008 | tf_op jit(solution)/shard_map/reshape;squeeze | solution.py:38
  23.3 0.4 copy.14
  23.7 16.1 %all-gather.1 = bf16[1,16,128,128]{3,2,0,1:T(8,128)(2,1)S(1)} all-gather(bf16[1,4,128,128]{3,2,0,1:T(8,128)(2,1)} %bitcast.40), channel_id=3, replica_groups=mesh['section'=2,'fsdp'=4,'dp'=4] {'fsdp'}, dimensions={1}, use_global_device_ids=true | all-gather | bytes 655360 | tf_op jit(solution)/shard_map/all_gather | solution.py:72
  39.8 5.9 %copy.20 = f32[16,8,112,128]{3,2,1,0:T(8,128)} copy(bf16[16,8,112,128]{3,1,2,0:T(8,128)(2,1)} %bitcast.38) | data formatting | bytes 11010048
  45.7 0.6 gather_fusion.1
  46.3 0.4 fusion.6
  46.7 3.9 %broadcast_in_dim.46 = f32[128,112,128]{2,0,1:T(8,128)} broadcast(f32[]{:T(128)} %constant.23.clone.1), dimensions={} | broadcast | bytes 7340036 | tf_op jit(solution)/shard_map/broadcast_in_dim | solution.py:51
  50.6 3.4 %scatter_fusion = f32[128,112,128]{2,0,1:T(8,128)} fusion(f32[128,112,128]{2,0,1:T(8,128)} %broadcast_in_dim.46, s32[16]{0:T(128)S(1)} %get-tuple-element.10, f32[16,128,128]{2,1,0:T(8,128)S(1)} %fusion.6), kind=kCustom, calls=%fused_computation.3 | custom fusion | flops 262144 | bytes 3145792 | tf_op jit(solution)/shard_map/scatter-add | solution.py:49
  54.0 8.4 %fusion = bf16[128,112,128]{2,0,1:T(8,128)(2,1)} fusion(f32[128,112,128]{2,1,0:T(8,128)} %bitcast.37, f32[128,112,128]{2,0,1:T(8,128)} %scatter_fusion), kind=kLoop, calls=%fused_computation.6 | loop fusion | flops 16515072 | bytes 18350080 | tf_op jit(solution)/shard_map/convert_element_type | solution.py:55
  62.4 2.7 %gather_fusion.2 = bf16[16,128,128]{2,1,0:T(8,128)(2,1)S(1)} fusion(bf16[128,112,128]{2,0,1:T(8,128)(2,1)} %fusion, s32[1024]{0:T(1024)S(1)} %get-tuple-element.12), kind=kCustom, calls=%fused_computation.1.clone | custom fusion | bytes 1048640 | tf_op jit(solution)/shard_map/jit(_take)/gather | solution.py:62
  65.1 1.4 %fusion.1 = f32[16,128,128]{2,1,0:T(8,128)} fusion(bf16[16,128,128]{2,1,0:T(8,128)(2,1)S(1)} %gather_fusion.1, pred[16]{0:T(512)(128)(4,1)S(1)} %get-tuple-element.8, bf16[16,128,128]{2,1,0:T(8,128)(2,1)S(1)} %gather_fusion.2, pred[16]{0:T(512)(128)(4,1)S(1)} %get-tuple-element.4), kind=kOutput, calls=%fused_computation.8 | convolution fusion | flops 67633152 | bytes 2097184 | tf_op jit(solution)/shard_map/tbk,tbn->bkn/dot_general | solution.py:84
  66.5 0.0 reduce-scatter.2.cloned.1.call-update
  66.6 0.0 all-reduce.2.cloned.1.call-start
  66.6 0.5 fusion.3
  67.2 0.2 broadcast_in_dim.45
  67.4 1.6 %scatter_fusion.1 = f32[128,28,128]{2,0,1:T(8,128)S(1)} fusion(f32[128,28,128]{2,0,1:T(8,128)S(1)} %broadcast_in_dim.45, s32[16]{0:T(128)S(1)} %get-tuple-element.11, f32[16,128,128]{2,1,0:T(8,128)S(1)} %fusion.3), kind=kCustom, calls=%fused_computation.4 | custom fusion | flops 262144 | bytes 3145792 | tf_op jit(solution)/shard_map/scatter-add | solution.py:66
  69.0 0.1 convert_element_type.17
  69.1 0.6 copy.17
  69.8 0.5 reshape.27
  70.3 0.6 gather_fusion
  70.9 0.2 broadcast_select_fusion
  71.1 1.3 collective-permute-start
  72.4 20.7 %reduce-scatter.2.cloned.1.call-done = f32[4,128,128]{2,1,0:T(8,128)} async-done(((f32[16,128,128]{2,1,0:T(8,128)}), f32[4,128,128]{2,1,0:T(8,128)}) %reduce-scatter.2.cloned.1.call-update) | async-done | bytes 262160 | tf_op jit(solution)/shard_map/reduce_scatter | solution.py:83
  93.0 0.0 all-reduce.2.cloned.1.call-update
  93.1 0.0 collective-permute-done
  93.1 33.1 %all-reduce.2.cloned.1.call-done = f32[4,128,128]{2,1,0:T(8,128)} async-done(((f32[4,128,128]{2,1,0:T(8,128)}), f32[4,128,128]{2,1,0:T(8,128)}) %all-reduce.2.cloned.1.call-update) | async-done | bytes 262160 | tf_op jit(solution)/shard_map/psum | solution.py:89
  126.2 1.7 %multiply_bitcast_fusion = f32[1,4,128,128]{3,2,1,0:T(8,128)} fusion(f32[4,128,128]{2,1,0:T(8,128)} %all-reduce.2.cloned.1.call-done), kind=kLoop, calls=%fused_computation.19 | loop fusion | flops 65536 | bytes 524288 | tf_op jit(solution)/shard_map/broadcast_in_dim | solution.py:91
  127.9 0.9 copy.28
  (8 shorter events, 0.0 us)
Async XLA Ops:
  7.2 85.9 %reduce-scatter.2.cloned.1.call-start = ((), (), s32[]{:S(2)}) async-start(), calls=%async_computation.1 | async-start | bytes 1310720 | tf_op jit(solution)/shard_map/reduce_scatter | solution.py:83
  54.0 13.1 %copy-start = (s32[4]{0:T(128)S(1)}, s32[4]{0:T(128)}, u32[]{:S(2)}) copy-start(s32[4]{0:T(128)} %param.13) | copy-start | bytes 52
  66.6 59.6 %all-reduce.2.cloned.1.call-start = ((), (), s32[]{:S(2)}) async-start(), calls=%async_computation.2 | async-start | bytes 524288 | tf_op jit(solution)/shard_map/psum | solution.py:89
  71.1 22.0 %collective-permute-start = (bf16[4,32,3584]{2,1,0:T(8,128)(2,1)S(1)}, bf16[4,32,3584]{2,1,0:T(8,128)(2,1)S(1)}, u32[]{:S(2)}, u32[]{:S(2)}) collective-permute-start(bf16[4,32,3584]{2,1,0:T(8,128)(2,1)S(1)} %broadcast_select_fusion), channel_id=1, source_target_pairs={{16,0},{17,1},{18,2},{19,3},{20,4},{21,5},{22,6},{23,7},{24,8},{25... | collective-permute-start | bytes 2752520 | tf_op jit(solution)/shard_map/ppermute | solution.py:11
Sparse Core Ops, SparseCore 0:
  66.7 26.2 reduce-scatter.1
  95.4 30.7 all-reduce.1
where the time goes:
time: 136 us
  waiting for transfers between devices  53.8 us (40%)
  blocking collectives  29.7 us (22%)
  local copies, waits for them, and re-layouts  18.8 us (14%)
  other arithmetic  15.4 us (11%)
  between operations  14.2 us (10%)
  matrix products  2.29 us (2%)
  starting transfers between devices  1.37 us (1%)
    psum x1, waiting for transfers between devices, local(): summed = lax.psum(owned_grads, 'dp')  33.1 us
    reduce_scatter x1, waiting for transfers between devices, local(): lax.psum_scatter(jnp.einsum('tbk,tbn->bkn', rows_in, cols_in, preferred_e...  20.7 us
    all_gather x1, blocking collectives, local(): lax.all_gather(own_blocks, 'fsdp', axis=0, tiled=True)  16.1 us
    all_gather x1, blocking collectives, local(): all_indices = lax.all_gather(pattern[0], 'fsdp', axis=0, tiled=True)  13.6 us
    convert_element_type x1, other arithmetic, local(): (hidden_grad.astype(jnp.float32) * silu_slope(pre_act.reshape(tok_rows, -...  8.43 us
    unnamed x5, local copies, waits for them, and re-layouts  7.54 us
    broadcast_in_dim x1, local copies, waits for them, and re-layouts, local(): pre_zero = jnp.zeros((tok_rows, col_count, block_size), jnp.float32)  3.95 us
    scatter-add x1, other arithmetic, forward_step(): return running.at[:, indices[:, 1]].add(product)  3.38 us
  transfers between devices with their start and end apart: 3, of which 2 were waited for; matrix products, arithmetic and copies ran while one was open for 3% of the time, Pallas kernels for 0%

commit v1 on v0

--- a/solution.py
+++ b/solution.py
@@ -3,6 +3,12 @@
 import jax.numpy as jnp
 from jax import lax
 from jax.sharding import PartitionSpec as P
+
+
+def joined_along(blocks, dim):
+    blocks = jnp.moveaxis(blocks, 0, dim)
+    lengths = blocks.shape
+    return blocks.reshape(*lengths[:dim], lengths[dim] * lengths[dim + 1], *lengths[dim + 2 :])
 
 
 def passed_along(block, axis, distance):
@@ -38,7 +44,14 @@
     features = activations[0].reshape(tok_rows, row_count, block_size)
     hidden_grad = out_grad[0].reshape(tok_rows, out_grad.shape[3])
     own_blocks = blocks[0]
-    all_indices = lax.all_gather(pattern[0], "fsdp", axis=0, tiled=True)
+    length = lax.axis_size("fsdp")
+    ahead = [(i_2, (i_2 + 1) % length) for i_2 in range(length)]
+    pieces = [pattern[0]]
+    while len(pieces) < length:
+        pieces.append(lax.ppermute(pieces[-1], "fsdp", ahead))
+    position = lax.axis_index("fsdp")
+    pieces = jnp.stack(pieces)[(position - jnp.arange(length)) % length]
+    all_indices = joined_along(pieces, 0)
 
     def forward_step(running, shard_blocks, first_block):
         indices = lax.dynamic_slice_in_dim(all_indices, first_block, shard_blocks.shape[0], 0)

time: 136 us -> 136 us (level)
  blocking collectives: 29.7 us -> 15.6 us
  waiting for transfers between devices: 53.8 us -> 63.5 us
  starting transfers between devices: 1.37 us -> 4.82 us
  other arithmetic: 15.4 us -> 16.8 us
    all_gather x1 -> x0, blocking collectives: 13.6 us -> none  [local(): all_indices = lax.all_gather(pattern[0], 'fsdp', axis=0, tiled=True)]
    ppermute x0 -> x3, waiting for transfers between devices: none -> 10.4 us  [local(): pieces.append(lax.ppermute(pieces[-1], 'fsdp', ahead))]
    ppermute x0 -> x3, starting transfers between devices: none -> 3.45 us  [local(): pieces.append(lax.ppermute(pieces[-1], 'fsdp', ahead))]
    unnamed x5 -> x4, local copies, waits for them, and re-layouts: 7.54 us -> 6.76 us
  transfers between devices with their start and end apart: 3 -> 6, of which waited for: 2 -> 4; matrix products, arithmetic and copies ran while one was open for 3% -> 10% of each run, Pallas kernels for 0% -> 0%
where the time goes in v1:
time: 136 us
  waiting for transfers between devices  63.5 us (47%)
  local copies, waits for them, and re-layouts  18.6 us (14%)
  other arithmetic  16.8 us (12%)
  blocking collectives  15.6 us (11%)
  between operations  14.2 us (10%)
  starting transfers between devices  4.82 us (4%)
  matrix products  2.27 us (2%)
    psum x1, waiting for transfers between devices, local(): summed = lax.psum(owned_grads, 'dp')  33.1 us
    reduce_scatter x1, waiting for transfers between devices, local(): lax.psum_scatter(jnp.einsum('tbk,tbn->bkn', rows_in, cols_in, preferred_e...  19.9 us
    all_gather x1, blocking collectives, local(): lax.all_gather(own_blocks, 'fsdp', axis=0, tiled=True)  15.6 us
    ppermute x3, waiting for transfers between devices, local(): pieces.append(lax.ppermute(pieces[-1], 'fsdp', ahead))  10.4 us
    convert_element_type x1, other arithmetic, local(): (hidden_grad.astype(jnp.float32) * silu_slope(pre_act.reshape(tok_rows, -...  8.44 us
    unnamed x4, local copies, waits for them, and re-layouts  6.76 us
    broadcast_in_dim x1, local copies, waits for them, and re-layouts, local(): pre_zero = jnp.zeros((tok_rows, col_count, block_size), jnp.float32)  3.93 us
    ppermute x3, starting transfers between devices, local(): pieces.append(lax.ppermute(pieces[-1], 'fsdp', ahead))  3.45 us
  transfers between devices with their start and end apart: 6, of which 4 were waited for; matrix products, arithmetic and copies ran while one was open for 10% of the time, Pallas kernels for 0%

profile of v1, /device:TPU:0, one launch (start us, length us, event | category | flops | bytes accessed | tf_op | source)
XLA Modules:
  0.0 135.7 jit_solution(155801294314059352)
XLA Ops:
  7.2 3.1 %collective-permute-start = (s32[4,2]{0,1:T(2,128)}, s32[4,2]{0,1:T(2,128)S(1)}, u32[]{:S(2)}, u32[]{:S(2)}) collective-permute-start(s32[4,2]{0,1:T(2,128)} %bitcast.48), channel_id=1, source_target_pairs={{0,4},{4,8},{8,12},{12,0},{1,5},{5,9},{9,13},{13,1},{2,6},{6,10},{... | collective-permute-start | bytes 104 | tf_op jit(solution)/shard_map/ppermute | solution.py:51
  10.3 0.7 compare_select_fusion.5
  11.0 0.7 compare_and_fusion.2
  11.7 1.6 %reshape_squeeze.4 = bf16[128,28,128]{2,1,0:T(8,128)(2,1)S(1)} reshape(bf16[1,4,32,3584]{3,2,1,0:T(8,128)(2,1)} %param.9) | data formatting | bytes 1835008 | tf_op jit(solution)/shard_map/reshape;squeeze | solution.py:44
  13.3 0.4 copy.15
  13.7 15.6 %all-gather = bf16[1,16,128,128]{3,2,0,1:T(8,128)(2,1)S(1)} all-gather(bf16[1,4,128,128]{3,2,0,1:T(8,128)(2,1)} %bitcast.47), channel_id=2, replica_groups=mesh['section'=2,'fsdp'=4,'dp'=4] {'fsdp'}, dimensions={1}, use_global_device_ids=true | all-gather | bytes 655360 | tf_op jit(solution)/shard_map/all_gather | solution.py:85
  29.2 5.8 %copy.21 = f32[16,8,112,128]{3,2,1,0:T(8,128)} copy(bf16[16,8,112,128]{3,1,2,0:T(8,128)(2,1)} %bitcast.45) | data formatting | bytes 11010048
  35.1 0.3 collective-permute-start.1
  35.4 5.0 %collective-permute-done.1 = s32[4,2]{0,1:T(2,128)S(1)} collective-permute-done((s32[4,2]{0,1:T(2,128)S(1)}, s32[4,2]{0,1:T(2,128)S(1)}, u32[]{:S(2)}, u32[]{:S(2)}) %collective-permute-start.1) | collective-permute-done | bytes 64 | tf_op jit(solution)/shard_map/ppermute | solution.py:51
  40.5 5.4 %collective-permute-done.2 = s32[4,2]{0,1:T(2,128)S(1)} collective-permute-done((s32[4,2]{0,1:T(2,128)S(1)}, s32[4,2]{0,1:T(2,128)S(1)}, u32[]{:S(2)}, u32[]{:S(2)}) %collective-permute-start.2) | collective-permute-done | bytes 64 | tf_op jit(solution)/shard_map/ppermute | solution.py:51
  45.8 0.6 gather_fusion
  46.4 0.1 reshape.79
  46.5 0.6 gather_fusion.2
  47.2 0.4 fusion.6
  47.6 3.9 %broadcast_in_dim.47 = f32[128,112,128]{2,0,1:T(8,128)} broadcast(f32[]{:T(128)} %constant.42.clone.1), dimensions={} | broadcast | bytes 7340036 | tf_op jit(solution)/shard_map/broadcast_in_dim | solution.py:64
  51.5 3.4 %scatter_fusion = f32[128,112,128]{2,0,1:T(8,128)} fusion(f32[128,112,128]{2,0,1:T(8,128)} %broadcast_in_dim.47, s32[16]{0:T(128)S(1)} %get-tuple-element.10, f32[16,128,128]{2,1,0:T(8,128)S(1)} %fusion.6), kind=kCustom, calls=%fused_computation.4 | custom fusion | flops 262144 | bytes 3145792 | tf_op jit(solution)/shard_map/scatter-add | solution.py:62
  54.9 8.4 %fusion = bf16[128,112,128]{2,0,1:T(8,128)(2,1)} fusion(f32[128,112,128]{2,1,0:T(8,128)} %bitcast.44, f32[128,112,128]{2,0,1:T(8,128)} %scatter_fusion), kind=kLoop, calls=%fused_computation.7 | loop fusion | flops 16515072 | bytes 18350080 | tf_op jit(solution)/shard_map/convert_element_type | solution.py:68
  63.3 2.7 %gather_fusion.3 = bf16[16,128,128]{2,1,0:T(8,128)(2,1)S(1)} fusion(bf16[128,112,128]{2,0,1:T(8,128)(2,1)} %fusion, s32[1024]{0:T(1024)S(1)} %get-tuple-element.12), kind=kCustom, calls=%fused_computation.1.clone | custom fusion | bytes 1048640 | tf_op jit(solution)/shard_map/jit(_take)/gather | solution.py:75
  66.0 1.4 %fusion.1 = f32[16,128,128]{2,1,0:T(8,128)} fusion(bf16[16,128,128]{2,1,0:T(8,128)(2,1)S(1)} %gather_fusion.2, pred[16]{0:T(512)(128)(4,1)S(1)} %get-tuple-element.8, bf16[16,128,128]{2,1,0:T(8,128)(2,1)S(1)} %gather_fusion.3, pred[16]{0:T(512)(128)(4,1)S(1)} %get-tuple-element.4), kind=kOutput, calls=%fused_computation.9 | convolution fusion | flops 67633152 | bytes 2097184 | tf_op jit(solution)/shard_map/tbk,tbn->bkn/dot_general | solution.py:97
  67.5 0.5 fusion.3
  68.0 0.2 broadcast_in_dim.46
  68.2 1.6 %scatter_fusion.1 = f32[128,28,128]{2,0,1:T(8,128)S(1)} fusion(f32[128,28,128]{2,0,1:T(8,128)S(1)} %broadcast_in_dim.46, s32[16]{0:T(128)S(1)} %get-tuple-element.11, f32[16,128,128]{2,1,0:T(8,128)S(1)} %fusion.3), kind=kCustom, calls=%fused_computation.5 | custom fusion | flops 262144 | bytes 3145792 | tf_op jit(solution)/shard_map/scatter-add | solution.py:79
  69.8 0.1 convert_element_type.17
  70.0 0.6 copy.18
  70.6 0.5 reshape.80
  71.1 0.6 gather_fusion.1
  71.7 0.2 broadcast_select_fusion
  71.9 1.3 collective-permute-start.3
  73.2 19.9 %reduce-scatter.2.cloned.1.call-done = f32[4,128,128]{2,1,0:T(8,128)} async-done(((f32[16,128,128]{2,1,0:T(8,128)}), f32[4,128,128]{2,1,0:T(8,128)}) %reduce-scatter.2.cloned.1.call-update) | async-done | bytes 262160 | tf_op jit(solution)/shard_map/reduce_scatter | solution.py:96
  93.1 33.1 %all-reduce.2.cloned.1.call-done = f32[4,128,128]{2,1,0:T(8,128)} async-done(((f32[4,128,128]{2,1,0:T(8,128)}), f32[4,128,128]{2,1,0:T(8,128)}) %all-reduce.2.cloned.1.call-update) | async-done | bytes 262160 | tf_op jit(solution)/shard_map/psum | solution.py:102
  126.3 1.7 %multiply_bitcast_fusion = f32[1,4,128,128]{3,2,1,0:T(8,128)} fusion(f32[4,128,128]{2,1,0:T(8,128)} %all-reduce.2.cloned.1.call-done), kind=kLoop, calls=%fused_computation.20 | loop fusion | flops 65536 | bytes 524288 | tf_op jit(solution)/shard_map/broadcast_in_dim | solution.py:104
  127.9 0.9 copy.29
  (17 shorter events, 0.2 us)
Async XLA Ops:
  7.2 85.9 %reduce-scatter.2.cloned.1.call-start = ((), (), s32[]{:S(2)}) async-start(), calls=%async_computation.1 | async-start | bytes 1310720 | tf_op jit(solution)/shard_map/reduce_scatter | solution.py:96
  7.2 27.9 %collective-permute-start = (s32[4,2]{0,1:T(2,128)}, s32[4,2]{0,1:T(2,128)S(1)}, u32[]{:S(2)}, u32[]{:S(2)}) collective-permute-start(s32[4,2]{0,1:T(2,128)} %bitcast.48), channel_id=1, source_target_pairs={{0,4},{4,8},{8,12},{12,0},{1,5},{5,9},{9,13},{13,1},{2,6},{6,10},{... | collective-permute-start | bytes 104 | tf_op jit(solution)/shard_map/ppermute | solution.py:51
  11.7 34.2 %copy-start = (s32[1,4,2]{1,2,0:T(2,128)S(1)}, s32[1,4,2]{1,2,0:T(2,128)}, u32[]{:S(2)}) copy-start(s32[1,4,2]{1,2,0:T(2,128)} %param.12) | copy-start | bytes 100
  35.1 5.4 %collective-permute-start.1 = (s32[4,2]{0,1:T(2,128)S(1)}, s32[4,2]{0,1:T(2,128)S(1)}, u32[]{:S(2)}, u32[]{:S(2)}) collective-permute-start(s32[4,2]{0,1:T(2,128)S(1)} %collective-permute-done), channel_id=1, source_target_pairs={{0,4},{4,8},{8,12},{12,0},{1,5},{5,9},{9,13},{13,1},{2,6},{6,10},{... | collective-permute-start | bytes 104 | tf_op jit(solution)/shard_map/ppermute | solution.py:51
  40.5 5.4 %collective-permute-start.2 = (s32[4,2]{0,1:T(2,128)S(1)}, s32[4,2]{0,1:T(2,128)S(1)}, u32[]{:S(2)}, u32[]{:S(2)}) collective-permute-start(s32[4,2]{0,1:T(2,128)S(1)} %collective-permute-done.1), channel_id=1, source_target_pairs={{0,4},{4,8},{8,12},{12,0},{1,5},{5,9},{9,13},{13,1},{2,6},{6,10},{... | collective-permute-start | bytes 104 | tf_op jit(solution)/shard_map/ppermute | solution.py:51
  67.4 58.8 %all-reduce.2.cloned.1.call-start = ((), (), s32[]{:S(2)}) async-start(), calls=%async_computation.2 | async-start | bytes 524288 | tf_op jit(solution)/shard_map/psum | solution.py:102
  71.9 21.3 %collective-permute-start.3 = (bf16[4,32,3584]{2,1,0:T(8,128)(2,1)S(1)}, bf16[4,32,3584]{2,1,0:T(8,128)(2,1)S(1)}, u32[]{:S(2)}, u32[]{:S(2)}) collective-permute-start(bf16[4,32,3584]{2,1,0:T(8,128)(2,1)S(1)} %broadcast_select_fusion), channel_id=1, source_target_pairs={{16,0},{17,1},{18,2},{19,3},{20,4},{21,5},{22,6},{23,7},{24,8},{25... | collective-permute-start | bytes 2752520 | tf_op jit(solution)/shard_map/ppermute | solution.py:17
Sparse Core Ops, SparseCore 0:
  67.6 25.5 reduce-scatter.1
  95.4 30.7 all-reduce.1
